TPU v7x, 256 devices: a whole 4x4x8 slice. The times are simulated.
256 devices in a mesh: comp: 2 (over core), seq: 16 (over y_lo, z), tp: 8 (over y_hi, x).
Axes of the slice: x: 4, y: 4 (y_hi: 2, y_lo: 2; y = y_hi * 2 + y_lo), z: 8, core: 2. Of those that a mesh axis runs over, the one named last changes fastest.
Arguments:
- inputs: bfloat16 [2, 8, 2048, 3072], P('comp', None, ('seq', 'tp')), may hold values from -6 to 6
- modulation: float32 [2, 8, 3, 3072], P('comp'), may hold values from -4 to 4
- w_qkv: bfloat16 [2, 3072, 3, 3072], P('comp', None, None, 'tp'), may hold values from -0.108253175 to 0.108253175
- w_attn_out: bfloat16 [2, 3072, 3072], P('comp', 'tp'), may hold values from -0.109375 to 0.109375
- qk_gain: float32 [2, 2, 128], P('comp'), may hold values from 1 to 5
- final_mod: float32 [8, 2, 3072], replicated, may hold values from -4 to 4
- w_final: bfloat16 [3072, 64], replicated, may hold values from -0.109375 to 0.109375
- w_embed: bfloat16 [64, 3072], replicated, may hold values from -0.75 to 0.75
- latent: float32 [8, 64, 2048], P(None, None, ('seq', 'tp')), may hold values from -6 to 6
Outputs:
- handed: bfloat16 [2, 8, 2048, 3072], P('comp', None, ('seq', 'tp'))
- velocity: float32 [8, 64, 2048], P(None, None, ('seq', 'tp'))
- advanced: float32 [8, 64, 2048], P(None, None, ('seq', 'tp'))
All inputs are finite; a program needn't handle non-finite values.
Results may differ from a plain program's by a relative error of at most 0.011.
Values may be sent and summed in bfloat16 or wider, within the bound.
No kernel may reach another device: no remote copies, remote signals or barrier semaphores. Data moves between devices by JAX's collectives and lax.ppermute only.
A program may use at most 192 MiB of HBM per device.

v0:
```python
import jax
import jax.numpy as jnp
from jax import lax
from jax.sharding import PartitionSpec as P

step_size = 0.02
norm_eps = 1e-06


def broadcast(block, axis, owner):
    block = jnp.where(lax.axis_index(axis) == owner, block, jnp.zeros_like(block))
    return lax.psum(block, axis)


def shifted(block, axis, distance):
    devices = range(lax.axis_size(axis))
    route = [((i - distance) % len(devices), i) for i in devices]
    return lax.ppermute(block, axis, route)


def layer_norm(values):
    center = values - jnp.mean(values, -1, keepdims=True)
    return center * lax.rsqrt(jnp.mean(center * center, -1, keepdims=True) + norm_eps)


def rms_norm(values, norm_gain):
    return values * lax.rsqrt(jnp.mean(values * values, -1, keepdims=True) + norm_eps) * norm_gain


def body(inputs, modulation, w_qkv, w_attn_out, qk_gain, final_mod, w_final, w_embed, latent):
    head_dim = qk_gain.shape[2]
    x_rows = inputs[0]
    samples = x_rows.shape[0]
    mod_rows = modulation[0]
    x_float = x_rows.astype(jnp.float32)
    x_mod = (
        layer_norm(x_float) * (1.0 + mod_rows[:, 1, None, :]) + mod_rows[:, 0, None, :]
    ).astype(jnp.bfloat16)
    weights = w_qkv[0]
    local_width = weights.shape[2]
    heads_local = local_width // head_dim
    norm_gains = qk_gain[0]
    scaling = head_dim ** (-0.5)
    mixed_rows = jnp.einsum(
        "srd,dje->srje",
        lax.all_gather(x_mod, "tp", axis=1, tiled=True),
        weights,
        preferred_element_type=jnp.float32,
    )
    unpacked = mixed_rows.reshape(
        mixed_rows.shape[0], mixed_rows.shape[1], 3, heads_local, head_dim
    )
    project_queried = rms_norm(unpacked[:, :, 0], norm_gains[0])
    keyed_rows = rms_norm(unpacked[:, :, 1], norm_gains[1])
    projected = jnp.stack([project_queried, keyed_rows, unpacked[:, :, 2]], 2).astype(jnp.bfloat16)
    queried = projected[:, :, 0]
    query_count = queried.shape[1]
    pairs = projected[:, :, 1:]
    start_max = jnp.full((samples, query_count, heads_local), -1e30, jnp.float32)
    shard_piece = lax.all_gather(pairs, "seq", axis=1, tiled=True)
    run_max = start_max
    scores = (
        jnp.einsum(
            "sqhd,skhd->sqhk", queried, shard_piece[:, :, 0], preferred_element_type=jnp.float32
        )
        * scaling
    )
    new_max = jnp.maximum(run_max, jnp.max(scores, -1))
    weight = jnp.exp(scores - new_max[..., None])
    run_sum = jnp.sum(weight, -1)
    summed = jnp.einsum(
        "sqhk,skhd->sqhd",
        weight.astype(jnp.bfloat16),
        shard_piece[:, :, 1],
        preferred_element_type=jnp.float32,
    )
    run_acc = summed
    run_max, run_sum, run_acc = (new_max, run_sum, run_acc)
    attended = (
        (run_acc / run_sum[..., None])
        .astype(jnp.bfloat16)
        .reshape(samples, query_count, local_width)
    )
    partial_out = jnp.einsum(
        "sqe,ed->sqd", attended, w_attn_out[0], preferred_element_type=jnp.float32
    )
    branch = lax.psum_scatter(
        partial_out.astype(jnp.bfloat16), "tp", scatter_dimension=1, tiled=True
    ).astype(jnp.float32)
    output = (x_float + mod_rows[:, 2, None, :] * branch).astype(jnp.bfloat16)
    final_in = (
        layer_norm(output.astype(jnp.float32)) * (1.0 + final_mod[:, 1, None, :])
        + final_mod[:, 0, None, :]
    ).astype(jnp.bfloat16)
    velocity = jnp.einsum("srd,dc->scr", final_in, w_final, preferred_element_type=jnp.float32)
    advanced = latent + step_size * velocity
    last_comp = lax.axis_size("comp") - 1
    position = lax.axis_index("comp")
    shared = broadcast(
        jnp.stack([velocity, advanced]).astype(jnp.bfloat16), "comp", last_comp
    ).astype(jnp.float32)
    embedded = jnp.einsum(
        "scr,cd->srd", advanced.astype(jnp.bfloat16), w_embed, preferred_element_type=jnp.float32
    ).astype(jnp.bfloat16)
    sending = jnp.where(position == last_comp, embedded, output)
    handed = shifted(sending, "comp", 1)
    return (handed[None], shared[0], shared[1])


def solution(mesh):
    in_specs = (
        P("comp", None, ("seq", "tp"), None),
        P("comp", None, None, None),
        P("comp", None, None, "tp"),
        P("comp", "tp", None),
        P("comp", None, None),
        P(),
        P(),
        P(),
        P(None, None, ("seq", "tp")),
    )
    out_specs = (
        P("comp", None, ("seq", "tp"), None),
        P(None, None, ("seq", "tp")),
        P(None, None, ("seq", "tp")),
    )
    return jax.shard_map(body, mesh=mesh, in_specs=in_specs, out_specs=out_specs, check_vma=False)
```

profile of v0, /device:TPU:1, one launch (start us, length us, event | category | flops | bytes accessed | tf_op | source)
XLA Modules:
  0.0 560.2 jit_solution(11027929013083755858)
XLA Ops:
  7.2 0.0 all-gather.3.cloned.1.call-start
  7.2 1.2 slice_bitcast_fusion.7
  8.4 1.3 convert_reduce_fusion.1
  9.8 0.3 fusion.22
  10.1 1.3 fusion.25
  11.5 0.0 all-gather.5.cloned.1.call-start
  11.5 10.3 %copy.18 = bf16[1,3072,3,384]{1,3,2,0:T(8,128)(2,1)} copy(bf16[1,3072,3,384]{3,1,2,0:T(8,128)(2,1)} %param.11) | data formatting | bytes 14155776 | tf_op args[2]
  21.8 87.1 %all-gather.3.cloned.1.call-done = bf16[8,128,3072]{2,1,0:T(8,128)(2,1)} async-done(((bf16[8,16,3072]{2,1,0:T(8,128)(2,1)}), bf16[8,128,3072]{2,1,0:T(8,128)(2,1)}) %all-gather.3.cloned.1.call-update) | async-done | bytes 6291472 | tf_op jit(solution)/shard_map/all_gather | solution.py:46
  108.9 10.5 %fusion.8 = f32[8,128,3,3,128]{1,4,3,2,0:T(8,128)S(1)} fusion(bf16[3,3,128,3072,1]{3,2,1,0,4:T(8,128)(2,1)} %bitcast.110, bf16[8,128,3072]{2,1,0:T(8,128)(2,1)} %all-gather.3.cloned.1.call-done), kind=kOutput, calls=%fused_computation.11 | convolution fusion | flops 7247757312 | bytes 18087936 | tf_op jit(solution)/shard_map/srd,dje->srje/dot_general | solution.py:44
  119.4 0.4 multiply_reduce_fusion
  119.8 0.1 slice.102
  120.0 1.6 copy-done.2
  121.6 0.3 multiply_convert_fusion.1
  121.9 1.4 pad_maximum_fusion
  123.3 0.2 reduce-scatter.2.cloned.1.call-start
  123.6 264.5 %all-gather.5.cloned.1.call-done = bf16[8,2048,2,3,128]{1,4,3,2,0:T(8,128)(2,1)} async-done(((bf16[8,128,2,3,128]{1,4,3,2,0:T(8,128)(2,1)}), bf16[8,2048,2,3,128]{1,4,3,2,0:T(8,128)(2,1)}) %all-gather.5.cloned.1.call-update) | async-done | bytes 25165840 | tf_op jit(solution)/shard_map/all_gather | solution.py:60
  388.0 13.9 %bitcast_reduce_fusion = (f32[8,128,3]{1,2,0:T(4,128)S(1)}, f32[8,3,2048,128]{3,2,1,0:T(8,128)}) fusion(f32[8,128,3,3,128]{1,4,3,2,0:T(8,128)} %copy-done.2, f32[128]{0:T(128)S(1)} %get-tuple-element.14, f32[8,128,3]{1,2,0:T(4,128)S(1)} %add_rsqrt_fusion, bf16[8,2048,2,3,128]{1,4,3,2,0:T(8,128)(2,1)} %all-gather.5.cloned.1.call-done), kind=kOutput, calls=%fused_computation.1 | convolution fusion | flops 1624372224 | bytes 39346688 | tf_op jit(solution)/shard_map/sqhd,skhd->sqhk/dot_general | solution.py:63
  402.0 10.5 %fusion.1 = f32[8,128,3]{1,2,0:T(4,128)S(1)} fusion(f32[8,3,2048,128]{3,2,1,0:T(8,128)} %get-tuple-element.17, f32[8,128,3]{1,2,0:T(4,128)S(1)} %broadcast_maximum_fusion), kind=kLoop, calls=%fused_computation.3 | loop fusion | flops 18871296 | bytes 25190400 | tf_op jit(solution)/shard_map/reduce_sum | solution.py:70
  412.4 15.2 %fusion.27 = bf16[8,128,3,128]{1,3,2,0:T(8,128)(2,1)S(1)} fusion(f32[8,3,2048,128]{3,2,1,0:T(8,128)} %get-tuple-element.17, f32[8,128,3]{1,2,0:T(4,128)S(1)} %broadcast_maximum_fusion, bf16[8,2048,2,3,128]{1,4,3,2,0:T(8,128)(2,1)} %all-gather.5.cloned.1.call-done, f32[8,128,3]{1,2,0:T(4,128)S(1)} %fusion.1), kind=kOutput, calls=%fused_computation.39 | convolution fusion | flops 1630273536 | bytes 38559744 | tf_op jit(solution)/shard_map/sqhk,skhd->sqhd/dot_general | solution.py:71
  427.6 5.4 convolution_convert_fusion
  433.1 0.9 copy-done.4
  433.9 0.2 fusion.43
  434.2 108.9 %reduce-scatter.2.cloned.1.call-done = bf16[8,16,3072]{2,1,0:T(8,128)(2,1)} async-done(((bf16[8,128,3072]{2,1,0:T(8,128)(2,1)}), bf16[8,16,3072]{2,1,0:T(8,128)(2,1)}) %reduce-scatter.2.cloned.1.call-update) | async-done | bytes 786448 | tf_op jit(solution)/shard_map/reduce_scatter | solution.py:87
  543.1 1.5 convert_reduce_fusion
  544.7 0.3 fusion.18
  545.0 0.5 fusion.40
  545.5 0.1 copy-done.3
  545.6 1.2 fusion.10
  546.9 1.6 collective-permute-start
  548.5 3.6 psum.7
  552.1 0.7 slice_bitcast_fusion.8
  552.8 0.9 copy.37
  (28 shorter events, 0.2 us)
Async XLA Ops:
  7.2 420.4 %copy-start = (bf16[1,384,3072]{2,1,0:T(8,128)(2,1)S(1)}, bf16[1,384,3072]{2,1,0:T(8,128)(2,1)}, u32[]{:S(2)}) copy-start(bf16[1,384,3072]{2,1,0:T(8,128)(2,1)} %param.12) | copy-start | bytes 7077892
  7.2 2.6 copy-start.1
  7.2 101.7 %all-gather.3.cloned.1.call-start = ((), (), s32[]{:S(2)}) async-start(), calls=%async_computation.1 | async-start | bytes 7077888 | tf_op jit(solution)/shard_map/all_gather | solution.py:46
  11.5 10.3 %copy-start.5 = (f32[1,2,128]{2,1,0:T(2,128)S(1)}, f32[1,2,128]{2,1,0:T(2,128)}, u32[]{:S(2)}) copy-start(f32[1,2,128]{2,1,0:T(2,128)} %param.13) | copy-start | bytes 3076
  11.5 376.6 %all-gather.5.cloned.1.call-start = ((), (), s32[]{:S(2)}) async-start(), calls=%async_computation.2 | async-start | bytes 26738688 | tf_op jit(solution)/shard_map/all_gather | solution.py:60
  119.4 2.2 copy-start.2
  123.3 419.8 %reduce-scatter.2.cloned.1.call-start = ((), (), s32[]{:S(2)}) async-start(), calls=%async_computation.3 | async-start | bytes 7077888 | tf_op jit(solution)/shard_map/reduce_scatter | solution.py:87
  433.0 0.9 copy-start.4
  543.1 1.9 copy-start.6
  543.1 1.9 copy-start.7
  544.6 1.0 copy-start.3
  546.9 5.9 %collective-permute-start = (bf16[8,16,3072]{2,1,0:T(8,128)(2,1)}, bf16[8,16,3072]{2,1,0:T(8,128)(2,1)S(1)}, u32[]{:S(2)}, u32[]{:S(2)}) collective-permute-start(bf16[8,16,3072]{2,1,0:T(8,128)(2,1)} %fusion.10), channel_id=1, source_target_pairs={{128,0},{0,128},{129,1},{1,129},{130,2},{2,130},{131,3},{3,131},{1... | collective-permute-start | bytes 2359304 | tf_op jit(solution)/shard_map/ppermute | solution.py:18
Sparse Core Ops, SparseCore 0:
  11.6 97.2 all-gather.2
  123.4 264.5 all-gather.4
  433.2 109.8 reduce-scatter.1
where the time goes:
time: 561 us; the launch traced here: 560 us
  waiting for transfers between devices  461 us (82%)
  matrix products  46.8 us (8%)
  other arithmetic  18.7 us (3%)
  local copies, waits for them, and re-layouts  14.8 us (3%)
  between operations  13.9 us (2%)
    all_gather x1, waiting for transfers between devices, body(): shard_piece = lax.all_gather(pairs, 'seq', axis=1, tiled=True)  264 us
    reduce_scatter x1, waiting for transfers between devices, body(): lax.psum_scatter(partial_out.astype(jnp.bfloat16), 'tp', scatter_dimensio...  109 us
    all_gather x1, waiting for transfers between devices, body(): lax.all_gather(x_mod, 'tp', axis=1, tiled=True)  87.1 us
    dot_general x1, matrix products, body(): jnp.einsum('sqhk,skhd->sqhd', weight.astype(jnp.bfloat16), shard_piece[:,...  15.2 us
    dot_general x1, matrix products, body(): jnp.einsum('sqhd,skhd->sqhk', queried, shard_piece[:, :, 0], preferred_el...  13.9 us
    unnamed x18, local copies, waits for them, and re-layouts  13.8 us
  transfers between devices with their start and end apart: 4, of which 3 were waited for; matrix products, arithmetic and copies ran while one was open for 2% of the time, Pallas kernels for 0%

commit v1 on v0

--- a/solution.py
+++ b/solution.py
@@ -57,7 +57,16 @@
     query_count = queried.shape[1]
     pairs = projected[:, :, 1:]
     start_max = jnp.full((samples, query_count, heads_local), -1e30, jnp.float32)
-    shard_piece = lax.all_gather(pairs, "seq", axis=1, tiled=True)
+    step_on_sides = lambda local_values, mesh_name, pos_dim: jnp.concatenate(
+        lax.all_to_all(
+            jnp.stack([local_values for _ in range(lax.psum(1, mesh_name))], axis=0),
+            mesh_name,
+            0,
+            0,
+        ),
+        axis=pos_dim,
+    )
+    shard_piece = step_on_sides(pairs, "seq", 1)
     run_max = start_max
     scores = (
         jnp.einsum(

time: 561 us -> 870 us (1.55)
  blocking collectives: 3.59 us -> 552 us
  waiting for transfers between devices: 461 us -> 187 us
  local copies, waits for them, and re-layouts: 14.8 us -> 47.9 us
    all_to_all x0 -> x1, blocking collectives: none -> 548 us  [body(): lax.all_to_all(jnp.stack([local_values for _ in range(lax.psum(1, mesh_na...]
    all_gather x1 -> x0, waiting for transfers between devices: 264 us -> none  [body(): shard_piece = lax.all_gather(pairs, 'seq', axis=1, tiled=True)]
    reshape x0 -> x1, local copies, waits for them, and re-layouts: none -> 23.2 us  [body(): jnp.concatenate(lax.all_to_all(jnp.stack([local_values for _ in range(lax...]
    another operation x0 -> x2, local copies, waits for them, and re-layouts: none -> 9.91 us  [the longest x1 7.31 us: body(): jnp.stack([local_values for _ in range(lax.psum(1, mesh_name))], axis=0)]
    reduce_scatter x1, waiting for transfers between devices: 109 us -> 100 us  [body(): lax.psum_scatter(partial_out.astype(jnp.bfloat16), 'tp', scatter_dimensio...]
  transfers between devices with their start and end apart: 4 -> 3, of which waited for: 3 -> 2; matrix products, arithmetic and copies ran while one was open for 2% -> 1% of each run, Pallas kernels for 0% -> 0%
where the time goes in v1:
time: 870 us
  blocking collectives  552 us (63%)
  waiting for transfers between devices  187 us (21%)
  matrix products  48.2 us (6%)
  local copies, waits for them, and re-layouts  47.9 us (6%)
  other arithmetic  18.6 us (2%)
  between operations  14.2 us (2%)
    all_to_all x1, blocking collectives, body(): lax.all_to_all(jnp.stack([local_values for _ in range(lax.psum(1, mesh_na...  548 us
    reduce_scatter x1, waiting for transfers between devices, body(): lax.psum_scatter(partial_out.astype(jnp.bfloat16), 'tp', scatter_dimensio...  100 us
    all_gather x1, waiting for transfers between devices, body(): lax.all_gather(x_mod, 'tp', axis=1, tiled=True)  87.1 us
    reshape x1, local copies, waits for them, and re-layouts, body(): jnp.concatenate(lax.all_to_all(jnp.stack([local_values for _ in range(lax...  23.2 us
  transfers between devices with their start and end apart: 3, of which 2 were waited for; matrix products, arithmetic and copies ran while one was open for 1% of the time, Pallas kernels for 0%

profile of v1, /device:TPU:1, one launch (start us, length us, event | category | flops | bytes accessed | tf_op | source)
XLA Modules:
  0.0 869.6 jit_solution(3249893844396708251)
XLA Ops:
  7.2 1.2 slice_bitcast_fusion.7
  8.4 1.3 convert_reduce_fusion.1
  9.8 0.3 fusion.22
  10.1 1.3 fusion.25
  11.5 10.3 %copy.27 = bf16[1,3072,3,384]{1,3,2,0:T(8,128)(2,1)} copy(bf16[1,3072,3,384]{3,1,2,0:T(8,128)(2,1)} %param.11) | data formatting | bytes 14155776 | tf_op args[2]
  21.8 87.1 %all-gather.2.cloned.1.call-done = bf16[8,128,3072]{2,1,0:T(8,128)(2,1)} async-done(((bf16[8,16,3072]{2,1,0:T(8,128)(2,1)}), bf16[8,128,3072]{2,1,0:T(8,128)(2,1)}) %all-gather.2.cloned.1.call-update) | async-done | bytes 6291472 | tf_op jit(solution)/shard_map/all_gather | solution.py:46
  108.9 10.5 %fusion.8 = f32[8,128,3,3,128]{1,4,3,2,0:T(8,128)S(1)} fusion(bf16[3,3,128,3072,1]{3,2,1,0,4:T(8,128)(2,1)} %bitcast.115, bf16[8,128,3072]{2,1,0:T(8,128)(2,1)} %all-gather.2.cloned.1.call-done), kind=kOutput, calls=%fused_computation.11 | convolution fusion | flops 7247757312 | bytes 18087936 | tf_op jit(solution)/shard_map/srd,dje->srje/dot_general | solution.py:44
  119.4 0.4 multiply_reduce_fusion
  119.8 0.1 slice.102
  120.0 1.6 copy-done.2
  121.6 0.3 multiply_convert_fusion.1
  121.9 1.3 pad_maximum_fusion
  123.2 2.6 copy.28
  125.8 7.3 stack.15
  133.1 548.3 %all_to_all.5 = bf16[16,8,128,2,3,128]{5,2,4,1,3,0:T(8,128)(2,1)} all-to-all(bf16[16,8,128,2,3,128]{5,2,4,1,3,0:T(8,128)(2,1)S(1)} %stack.15), channel_id=1, replica_groups=mesh['comp'=2,'seq'=16,'tp'=8] {'seq'}, dimensions={0} | all-to-all | bytes 50331648 | tf_op jit(solution)/shard_map/all_to_all | solution.py:61
  681.4 23.2 %copy.29 = bf16[8,16,128,2,3,128]{5,2,1,4,0,3:T(8,128)(2,1)} copy(bf16[8,16,128,2,3,128]{5,2,4,0,3,1:T(8,128)(2,1)} %bitcast.112) | data formatting | bytes 50331648 | tf_op jit(solution)/shard_map/reshape | solution.py:60
  704.6 13.3 %bitcast_reduce_fusion = (f32[8,128,3]{1,2,0:T(4,128)S(1)}, f32[8,3,2048,128]{3,2,1,0:T(8,128)}) fusion(f32[8,128,3,3,128]{1,4,3,2,0:T(8,128)} %copy-done.2, f32[128]{0:T(128)S(1)} %get-tuple-element.14, f32[8,128,3]{1,2,0:T(4,128)S(1)} %get-tuple-element.20, bf16[8,2048,2,3,128]{4,1,3,0,2:T(8,128)(2,1)} %bitcast.113), kind=kOutput, calls=%fused_computation.1 | convolution fusion | flops 1624372224 | bytes 39346688 | tf_op jit(solution)/shard_map/sqhd,skhd->sqhk/dot_general | solution.py:72
  718.0 10.5 %fusion.1 = f32[8,128,3]{1,2,0:T(4,128)S(1)} fusion(f32[8,3,2048,128]{3,2,1,0:T(8,128)} %get-tuple-element.17, f32[8,128,3]{1,2,0:T(4,128)S(1)} %broadcast_maximum_fusion), kind=kLoop, calls=%fused_computation.3 | loop fusion | flops 18871296 | bytes 25190400 | tf_op jit(solution)/shard_map/reduce_sum | solution.py:79
  728.4 16.2 %fusion.27 = bf16[8,128,3,128]{1,3,2,0:T(8,128)(2,1)} fusion(f32[8,3,2048,128]{3,2,1,0:T(8,128)} %get-tuple-element.17, f32[8,128,3]{1,2,0:T(4,128)S(1)} %broadcast_maximum_fusion, bf16[8,2048,2,3,128]{4,1,3,0,2:T(8,128)(2,1)} %bitcast.114, f32[8,128,3]{1,2,0:T(4,128)S(1)} %fusion.1), kind=kOutput, calls=%fused_computation.39 | convolution fusion | flops 1630273536 | bytes 38559744 | tf_op jit(solution)/shard_map/sqhk,skhd->sqhd/dot_general | solution.py:80
  744.6 6.5 convolution_convert_fusion
  751.1 0.9 copy-done.4
  752.0 0.2 fusion.43
  752.2 100.0 %reduce-scatter.2.cloned.1.call-done = bf16[8,16,3072]{2,1,0:T(8,128)(2,1)} async-done(((bf16[8,128,3072]{2,1,0:T(8,128)(2,1)}), bf16[8,16,3072]{2,1,0:T(8,128)(2,1)}) %reduce-scatter.2.cloned.1.call-update) | async-done | bytes 786448 | tf_op jit(solution)/shard_map/reduce_scatter | solution.py:96
  852.3 1.5 convert_reduce_fusion
  853.8 0.3 fusion.18
  854.2 0.5 fusion.40
  854.7 0.1 copy-done.3
  854.8 1.2 fusion.10
  856.0 1.6 collective-permute-start
  857.6 3.6 psum.7
  861.3 0.7 slice_bitcast_fusion.8
  861.9 0.9 copy.48
  (28 shorter events, 0.3 us)
Async XLA Ops:
  7.2 737.4 %copy-start = (bf16[1,384,3072]{2,1,0:T(8,128)(2,1)S(1)}, bf16[1,384,3072]{2,1,0:T(8,128)(2,1)}, u32[]{:S(2)}) copy-start(bf16[1,384,3072]{2,1,0:T(8,128)(2,1)} %param.12) | copy-start | bytes 7077892
  7.2 2.6 copy-start.1
  7.2 101.7 %all-gather.2.cloned.1.call-start = ((), (), s32[]{:S(2)}) async-start(), calls=%async_computation.2 | async-start | bytes 7077888 | tf_op jit(solution)/shard_map/all_gather | solution.py:46
  11.5 10.3 %copy-start.5 = (f32[1,2,128]{2,1,0:T(2,128)S(1)}, f32[1,2,128]{2,1,0:T(2,128)}, u32[]{:S(2)}) copy-start(f32[1,2,128]{2,1,0:T(2,128)} %param.13) | copy-start | bytes 3076
  11.5 840.8 %reduce-scatter.2.cloned.1.call-start = ((), (), s32[]{:S(2)}) async-start(), calls=%async_computation.3 | async-start | bytes 7077888 | tf_op jit(solution)/shard_map/reduce_scatter | solution.py:96
  119.4 2.2 copy-start.2
  751.1 0.9 copy-start.4
  852.3 1.9 copy-start.6
  852.3 1.9 copy-start.7
  853.8 1.0 copy-start.3
  856.0 5.9 collective-permute-start
Sparse Core Ops, SparseCore 0:
  11.6 97.2 all-gather.1
  751.2 100.9 reduce-scatter.1
